TPU v7x, 128 devices: a whole 4x4x4 slice. The times are simulated.
128 devices in a mesh: req: 16 (over y, z), mp: 8 (over x, core).
Axes of the slice: x: 4, y: 4, z: 4, core: 2. Of those that a mesh axis runs over, the one named last changes fastest.
Arguments:
- hidden_in: bfloat16 [16384, 2048], P('req', 'mp'), may hold values from -6 to 6
- w_qkv: bfloat16 [3, 2048, 2048], P(None, 'req', 'mp'), may hold values from -0.125 to 0.125
- w_out: bfloat16 [2048, 2048], P('mp', 'req'), may hold values from -0.125 to 0.125
- attn_gain: bfloat16 [2048], replicated, may hold values from 0.099609375 to 1.8984375
- mlp_gain: bfloat16 [2048], replicated, may hold values from 0.099609375 to 1.8984375
- w_gate: bfloat16 [2048, 8192], P('req', 'mp'), may hold values from -0.125 to 0.125
- w_up: bfloat16 [2048, 8192], P('req', 'mp'), may hold values from -0.125 to 0.125
- w_down: bfloat16 [8192, 2048], P('mp', 'req'), may hold values from -0.0625 to 0.0625
- k_cache: bfloat16 [16, 4096, 2048], P('req', None, 'mp'), may hold values from -363 to 363
- v_cache: bfloat16 [16, 4096, 2048], P('req', None, 'mp'), may hold values from -6 to 6
- cache_len: int32 [16], P('req'), may hold values from 256 to 4096, as said below
Outputs:
- hidden_out: bfloat16 [16384, 2048], P('req', 'mp')
- new_keys: bfloat16 [16384, 2048], P('req', 'mp')
- new_values: bfloat16 [16384, 2048], P('req', 'mp')
Inputs may be any that keep to these rules, and one draw needn't show every extreme that they name: Each request uses its first cache_len slots; later slots hold unused data. Some request's cache is full in every draw.
All inputs are finite; a program needn't handle non-finite values.
Results may differ from a plain program's by a relative error of at most 0.02.
Values may be sent and summed in bfloat16 or wider, within the bound.
No kernel may reach another device: no remote copies, remote signals or barrier semaphores. Data moves between devices by JAX's collectives and lax.ppermute only.
A program may use at most 128 MiB of HBM per device.

v0:
```python
import jax
import jax.numpy as jnp
from jax import lax
from jax.sharding import PartitionSpec as P

HD = 64
THETA = 130000.0
EPSILON = 1e-05
NEG_FILL = -1e30


def rms_scale(rows, gain):
    values = rows.astype(jnp.float32)
    meansq = jnp.mean(values * values, axis=-1, keepdims=True)
    return (values * lax.rsqrt(meansq + EPSILON) * gain.astype(jnp.float32)).astype(jnp.bfloat16)


def rotate(tensor, positions):
    half = tensor.shape[-1] // 2
    freq = THETA ** (-(jnp.arange(half, dtype=jnp.float32) * 2.0 / tensor.shape[-1]))
    angle = positions[:, None, None] * freq[None, None, :]
    cosine = jnp.cos(angle)
    sine = jnp.sin(angle)
    first = tensor[..., :half]
    second = tensor[..., half:]
    return jnp.concatenate(
        [first * cosine - second * sine, second * cosine + first * sine], axis=-1
    )


def gather_packed(blocks, axes, axis_name):
    count = lax.axis_size(axis_name)
    lane = 128
    joined = jnp.concatenate([block.reshape(-1, lane) for block in blocks], axis=0)
    gathered = lax.all_gather(joined, axis_name, axis=0, tiled=False)
    outs = []
    offset = 0
    for block, axis in zip(blocks, axes):
        rows = block.size // lane
        piece = gathered[:, offset : offset + rows].reshape((count,) + block.shape)
        piece = jnp.moveaxis(piece, 0, axis)
        shape = list(block.shape)
        shape[axis] *= count
        outs.append(piece.reshape(shape))
        offset += rows
    return outs


def absorb(carry, queries, keys, values, valid):
    top, total, accum = carry
    scores = jnp.einsum("qhd,khd->hqk", queries, keys, preferred_element_type=jnp.float32) * HD ** (
        -0.5
    )
    scores = jnp.where(valid[None], scores, NEG_FILL)
    new_top = jnp.maximum(top, jnp.max(scores, axis=-1, keepdims=True))
    factor = jnp.exp(top - new_top)
    probs = jnp.where(valid[None], jnp.exp(scores - new_top), 0.0)
    total = total * factor + jnp.sum(probs, axis=-1, keepdims=True)
    accum = accum * factor + jnp.einsum(
        "hqk,khd->hqd", probs.astype(jnp.bfloat16), values, preferred_element_type=jnp.float32
    )
    return (new_top, total, accum)


def on_device(
    hidden_in, w_qkv, w_out, attn_gain, mlp_gain, w_gate, w_up, w_down, k_cache, v_cache, cache_len
):
    new_count = hidden_in.shape[0]
    w_qkv_full = lax.all_gather(w_qkv, "req", axis=1, tiled=True)
    w_gate_full, w_up_full, w_down_full, w_out_full = gather_packed(
        [w_gate, w_up, w_down, w_out], [0, 0, 1, 1], "req"
    )
    width = w_qkv.shape[2]
    heads_local = width // HD
    slots = k_cache.shape[1]
    full_rows = lax.all_gather(hidden_in, "mp", axis=1, tiled=True)
    normed = rms_scale(full_rows, attn_gain)
    columns = normed
    projected = jnp.einsum("nd,kdw->knw", columns, w_qkv_full, preferred_element_type=jnp.float32)
    length = cache_len[0]
    positions = (length + jnp.arange(new_count, dtype=jnp.int32)).astype(jnp.float32)
    queries = rotate(projected[0].reshape(new_count, heads_local, HD), positions).astype(
        jnp.bfloat16
    )
    fresh_keys = rotate(projected[1].reshape(new_count, heads_local, HD), positions).astype(
        jnp.bfloat16
    )
    fresh_values = projected[2].astype(jnp.bfloat16).reshape(new_count, heads_local, HD)
    rows = jnp.arange(new_count, dtype=jnp.int32)
    causal = rows[:, None] >= rows[None, :]
    start_carry = (
        jnp.full((heads_local, new_count, 1), NEG_FILL, jnp.float32),
        jnp.zeros((heads_local, new_count, 1), jnp.float32),
        jnp.zeros((heads_local, new_count, HD), jnp.float32),
    )
    carry = absorb(start_carry, queries, fresh_keys, fresh_values, causal)
    cache_keys = k_cache[0].reshape(slots, heads_local, HD)
    cache_values = v_cache[0].reshape(slots, heads_local, HD)
    block = min(slots, 512)
    count = (length + block - 1) // block

    def step_block(index, state):
        begin = index * block
        keys = lax.dynamic_slice_in_dim(cache_keys, begin, block, 0)
        values = lax.dynamic_slice_in_dim(cache_values, begin, block, 0)
        valid = (begin + jnp.arange(block, dtype=jnp.int32) < length)[None, :]
        return absorb(state, queries, keys, values, valid)

    top, total, accum = lax.fori_loop(0, count, step_block, carry)
    attn = (accum / total).transpose(1, 0, 2).reshape(new_count, width).astype(jnp.bfloat16)
    partial_value = jnp.dot(attn, w_out_full, preferred_element_type=jnp.float32)
    summed = lax.psum(partial_value.astype(jnp.bfloat16), "mp").astype(jnp.float32)
    mid_full = (full_rows.astype(jnp.float32) + summed).astype(jnp.bfloat16)
    own = hidden_in.shape[1]
    mid_local = lax.dynamic_slice_in_dim(mid_full, lax.axis_index("mp") * own, own, axis=1)
    normed2 = rms_scale(mid_full, mlp_gain)
    columns = normed2
    gate = jnp.dot(columns, w_gate_full, preferred_element_type=jnp.float32)
    upper = jnp.dot(columns, w_up_full, preferred_element_type=jnp.float32)
    units = (jax.nn.silu(gate) * upper).astype(jnp.bfloat16)
    terms = jnp.dot(units, w_down_full, preferred_element_type=jnp.float32)
    reduced = lax.psum_scatter(
        terms.astype(jnp.bfloat16), "mp", scatter_dimension=1, tiled=True
    ).astype(jnp.float32)
    hidden_out = (mid_local.astype(jnp.float32) + reduced).astype(jnp.bfloat16)
    return (
        hidden_out,
        fresh_keys.reshape(new_count, width),
        fresh_values.reshape(new_count, width),
    )


def solution(mesh):
    return jax.shard_map(
        on_device,
        mesh=mesh,
        in_specs=(
            P("req", "mp"),
            P(None, "req", "mp"),
            P("mp", "req"),
            P(),
            P(),
            P("req", "mp"),
            P("req", "mp"),
            P("mp", "req"),
            P("req", None, "mp"),
            P("req", None, "mp"),
            P("req"),
        ),
        out_specs=(P("req", "mp"), P("req", "mp"), P("req", "mp")),
        check_vma=False,
    )
```

profile of v0, /device:TPU:0, one launch (start us, length us, event | category | flops | bytes accessed | tf_op | source)
XLA Modules:
  0.0 353.1 jit_solution(15132475671423839923)
XLA Ops:
  7.2 0.0 copy-start.7
  7.2 0.0 all-gather.5.cloned.1.call-start
  7.2 0.7 all-gather.5.cloned.1.call-update
  7.9 0.0 all-gather.7.cloned.1.call-start
  8.0 1.7 copy.29
  9.7 0.0 all-gather.7.cloned.1.call-update
  9.7 0.0 all-gather.9.cloned.1.call-start
  9.8 1.1 reshape.167
  10.8 1.1 reshape.168
  11.9 2.0 pad_maximum_fusion
  13.9 0.0 all-gather.9.cloned.1.call-update
  13.9 0.0 all-reduce.2.cloned.1.call-start
  14.6 0.0 copy-done.7
  14.6 2.9 copy.31
  17.6 4.1 %copy.32 = bf16[1,4096,256]{1,2,0:T(8,128)(2,1)} copy(bf16[1,4096,256]{2,1,0:T(8,128)(2,1)} %param.22) | data formatting | bytes 4194304 | tf_op args[9]
  21.7 1.3 iota_compare_fusion
  23.0 0.5 multiply_cosine_fusion
  23.5 24.7 %all-gather.5.cloned.1.call-done = bf16[1024,2048]{1,0:T(8,128)(2,1)} async-done(((bf16[1024,256]{1,0:T(8,128)(2,1)}), bf16[1024,2048]{1,0:T(8,128)(2,1)}) %all-gather.5.cloned.1.call-update) | async-done | bytes 4194320 | tf_op jit(solution)/shard_map/all_gather | solution.py:76
  48.2 3.1 fusion.26
  51.3 53.4 %all-gather.7.cloned.1.call-done = bf16[3,2048,256]{1,2,0:T(8,128)(2,1)} async-done(((bf16[3,128,256]{1,2,0:T(8,128)(2,1)}), bf16[3,2048,256]{1,2,0:T(8,128)(2,1)}) %all-gather.7.cloned.1.call-update) | async-done | bytes 3145744 | tf_op jit(solution)/shard_map/all_gather | solution.py:69
  104.7 6.6 %fusion.38 = f32[3,1024,256]{1,2,0:T(8,128)S(1)} fusion(bf16[3,2048,256]{1,2,0:T(8,128)(2,1)} %all-gather.7.cloned.1.call-done, bf16[1024,2048]{1,0:T(8,128)(2,1)} %all-gather.5.cloned.1.call-done, f32[2048]{0:T(1024)S(1)} %convert_element_type.84, f32[1024]{0:T(1024)S(1)} %add_rsqrt_fusion.1), kind=kOutput, calls=%fused_computation.52 | convolution fusion | flops 3229614080 | bytes 10498048 | tf_op jit(solution)/shard_map/nd,kdw->knw/dot_general | solution.py:79
  111.3 0.0 copy-start.3
  111.3 1.0 slice.66
  112.3 0.1 fusion.57
  112.4 0.2 subtract_convert_fusion
  112.6 0.2 multiply_subtract_fusion
  112.8 0.3 copy-done.3
  113.1 0.7 copy-done.1
  113.8 3.0 fusion.20
  116.8 0.0 copy-start.6
  116.8 4.2 %fusion.22 = f32[4,1024]{1,0:T(4,128)S(1)} fusion(f32[4,1024,1024]{1,2,0:T(8,128)S(1)} %get-tuple-element.102, f32[4,1024]{1,0:T(4,128)S(1)} %get-tuple-element.98, pred[1024,1024]{0,1:T(8,128)(4,1)S(1)} %copy-done.1), kind=kLoop, calls=%fused_computation.31 | loop fusion | flops 20967424 | bytes 17858560 | tf_op jit(solution)/shard_map/reduce_sum | solution.py:58
  121.1 0.0 copy-done.6
  121.1 5.9 %fusion.41 = f32[4,1024,64]{1,2,0:T(8,128)} fusion(bf16[1024,4,64]{0,2,1:T(8,128)(2,1)S(1)} %bitcast.91, f32[4,1024,1024]{1,2,0:T(8,128)S(1)} %get-tuple-element.102, f32[4,1024]{1,0:T(4,128)S(1)} %get-tuple-element.98, pred[1024,1024]{0,1:T(8,128)(4,1)S(1)} %copy-done.1, f32[4,1024]{1,0:T(4,128)S(1)} %get-tuple-element.96), kind=kOutput, calls=%fused_computation.53 | convolution fusion | flops 558104576 | bytes 19431424 | tf_op jit(solution)/shard_map/hqk,khd->hqd/dot_general | solution.py:59
  127.0 8.0 %while.14 = (s32[]{:T(128)}, f32[4,1024,1]{1,0,2:T(4,128)S(1)}, f32[4,1024,1]{1,0,2:T(4,128)S(1)}, f32[4,1024,64]{1,2,0:T(8,128)}, s32[]{:T(128)}, /*index=5*/s3...) while((s32[]{:T(128)}, f32[4,1024,1]{1,0,2:T(4,128)S(1)}, ...), condition=%wide.region_6.7_spmd, body=%wide.region_3.6_spmd.sunk | while | flops 564671488 | bytes 36965104 | solution.py:109
  127.0 0.7 add_compare_fusion.2
  127.7 0.0 copy-start.4
  127.7 1.6 bitcast_reduce_fusion.2
  129.3 0.0 copy-done.4
  129.3 3.1 fusion.77
  132.4 0.0 copy-start.5
  132.4 2.5 fusion.76
  135.0 1.3 divide_convert_fusion
  136.3 65.2 %all-gather.9.cloned.1.call-done = bf16[53248,128]{1,0:T(8,128)(2,1)} async-done(((bf16[3328,128]{1,0:T(8,128)(2,1)}), bf16[53248,128]{1,0:T(8,128)(2,1)}) %all-gather.9.cloned.1.call-update) | async-done | bytes 13631504 | tf_op jit(solution)/shard_map/all_gather | solution.py:35
  201.5 1.3 slice_bitcast_fusion.1
  202.8 0.5 copy.33
  203.4 3.3 convolution_convert_fusion
  206.7 0.0 all-reduce.2.cloned.1.call-update
  206.7 0.3 reduce-scatter.2.cloned.1.call-start
  207.0 0.4 copy-done.8
  207.4 9.1 %fusion.56 = (bf16[16,1024,128]{2,1,0:T(8,128)(2,1)}, bf16[1024,16,128]{2,0,1:T(8,128)(2,1)}, bf16[16,1024,128]{2,1,0:T(8,128)(2,1)}) fusion(bf16[16,3328,128]{2,1,0:T(8,128)(2,1)} %bitcast.79), kind=kLoop, calls=%fused_computation.81 | loop fusion | bytes 25165824 | tf_op jit(solution)/shard_map/slice | solution.py:40
  216.5 7.4 %reshape_reshape.6 = bf16[2048,1024]{1,0:T(8,128)(2,1)} reshape(bf16[16,1024,128]{2,1,0:T(8,128)(2,1)} %get-tuple-element.89) | data formatting | bytes 8388608 | tf_op jit(solution)/shard_map/reshape;reshape | solution.py:44
  223.9 6.4 %copy.34 = bf16[1024,16,128]{0,2,1:T(8,128)(2,1)} copy(bf16[1024,16,128]{2,0,1:T(8,128)(2,1)} %get-tuple-element.88) | data formatting | bytes 8388608 | tf_op jit(solution)/shard_map/transpose | solution.py:41
  230.4 7.4 %reshape_reshape.7 = bf16[2048,1024]{1,0:T(8,128)(2,1)} reshape(bf16[16,1024,128]{2,1,0:T(8,128)(2,1)} %get-tuple-element.87) | data formatting | bytes 8388608 | tf_op jit(solution)/shard_map/reshape;reshape | solution.py:44
  237.8 41.3 %all-reduce.2.cloned.1.call-done = bf16[1024,2048]{1,0:T(8,128)(2,1)} async-done(((bf16[1024,2048]{1,0:T(8,128)(2,1)}), bf16[1024,2048]{1,0:T(8,128)(2,1)}) %all-reduce.2.cloned.1.call-update) | async-done | bytes 4194320 | tf_op jit(solution)/shard_map/psum | solution.py:112
  279.0 5.6 %fusion.23 = (f32[1024]{0:T(1024)S(1)}, bf16[1024,2048]{1,0:T(8,128)(2,1)S(1)}) fusion(bf16[1024,2048]{1,0:T(8,128)(2,1)} %all-reduce.2.cloned.1.call-done, bf16[1024,2048]{1,0:T(8,128)(2,1)} %all-gather.5.cloned.1.call-done), kind=kLoop, calls=%fused_computation.34 | loop fusion | flops 14679040 | bytes 12587008 | tf_op jit(solution)/shard_map/reduce_sum | solution.py:14
  284.7 0.0 copy-done.2
  284.7 6.3 %fusion.45 = f32[1024,1024]{1,0:T(8,128)} fusion(bf16[2048,1024]{1,0:T(8,128)(2,1)S(1)} %copy-done.2, bf16[1024,2048]{1,0:T(8,128)(2,1)S(1)} %get-tuple-element.84, f32[2048]{0:T(1024)S(1)} %convert_element_type.99, f32[1024]{0:T(1024)S(1)} %add_rsqrt_fusion), kind=kOutput, calls=%fused_computation.54 | convolution fusion | flops 4303355904 | bytes 12595200 | tf_op jit(solution)/shard_map/dot_general | solution.py:118
  291.0 15.4 %convolution_convert_fusion.1 = bf16[1024,2048]{1,0:T(8,128)(2,1)} fusion(bf16[1024,2048]{0,1:T(8,128)(2,1)} %bitcast.84, f32[1024,1024]{1,0:T(8,128)} %fusion.45, bf16[2048,1024]{1,0:T(8,128)(2,1)} %reshape_reshape.7, bf16[1024,2048]{1,0:T(8,128)(2,1)} %copy-done, f32[2048]{0:T(1024)S(1)} %convert_element_type.99, f32[1024]{0:T(1024)S(1)} %add_rsqrt_fusion), kind=kOutput, calls=%fused_computation.51 | convolution fusion | flops 8606711808 | bytes 20983808 | tf_op jit(solution)/shard_map/dot_general | solution.py:121
  306.4 0.0 reduce-scatter.2.cloned.1.call-update
  306.4 1.0 copy.35
  307.4 1.3 slice_bitcast_fusion.2
  308.7 1.0 copy.36
  309.7 34.8 %reduce-scatter.2.cloned.1.call-done = bf16[1024,256]{1,0:T(8,128)(2,1)} async-done(((bf16[1024,2048]{1,0:T(8,128)(2,1)}), bf16[1024,256]{1,0:T(8,128)(2,1)}) %reduce-scatter.2.cloned.1.call-update) | async-done | bytes 524304 | tf_op jit(solution)/shard_map/reduce_scatter | solution.py:122
  344.5 2.1 add_convert_fusion
  (19 shorter events, 0.2 us)
Async XLA Ops:
  7.2 7.4 %copy-start.7 = (bf16[2048]{0:T(1024)(128)(2,1)S(1)}, bf16[2048]{0:T(1024)(128)(2,1)}, u32[]{:S(2)}) copy-start(bf16[2048]{0:T(1024)(128)(2,1)} %param.16) | copy-start | bytes 12292
  7.2 41.0 %all-gather.5.cloned.1.call-start = ((), (), s32[]{:S(2)}) async-start(), calls=%async_computation.1 | async-start | bytes 4718592 | tf_op jit(solution)/shard_map/all_gather | solution.py:76
  7.9 96.8 %all-gather.7.cloned.1.call-start = ((), (), s32[]{:S(2)}) async-start(), calls=%async_computation.2 | async-start | bytes 3342336 | tf_op jit(solution)/shard_map/all_gather | solution.py:69
  9.7 191.8 %all-gather.9.cloned.1.call-start = ((), (), s32[]{:S(2)}) async-start(), calls=%async_computation.5 | async-start | bytes 14483456 | tf_op jit(solution)/shard_map/all_gather | solution.py:35
  13.9 265.1 %all-reduce.2.cloned.1.call-start = ((), (), s32[]{:S(2)}) async-start(), calls=%async_computation.3 | async-start | bytes 8388608 | tf_op jit(solution)/shard_map/psum | solution.py:112
  111.3 1.8 copy-start.3
  112.3 1.5 copy-start.1
  116.8 4.2 %copy-start.6 = (bf16[1,1024,256]{1,2,0:T(8,128)(2,1)S(1)}, bf16[1,1024,256]{1,2,0:T(8,128)(2,1)}, u32[]{:S(2)}) copy-start(bf16[1,1024,256]{1,2,0:T(8,128)(2,1)} %slice.66) | copy-start | bytes 1572868
  127.7 1.6 copy-start.4
  132.4 2.6 copy-start.5
  206.7 0.7 copy-start.8
  206.7 137.7 %reduce-scatter.2.cloned.1.call-start = ((), (), s32[]{:S(2)}) async-start(), calls=%async_computation.4 | async-start | bytes 4718592 | tf_op jit(solution)/shard_map/reduce_scatter | solution.py:122
  279.0 5.6 %copy-start.2 = (bf16[2048,1024]{1,0:T(8,128)(2,1)S(1)}, bf16[2048,1024]{1,0:T(8,128)(2,1)}, u32[]{:S(2)}) copy-start(bf16[2048,1024]{1,0:T(8,128)(2,1)} %reshape_reshape.6) | copy-start | bytes 12582916
  284.6 6.4 %copy-start = (bf16[1024,2048]{1,0:T(8,128)(2,1)}, bf16[1024,2048]{1,0:T(8,128)(2,1)S(1)}, u32[]{:S(2)}) copy-start(bf16[1024,2048]{1,0:T(8,128)(2,1)S(1)} %get-tuple-element.84) | copy-start | bytes 12582916
Sparse Core Ops, SparseCore 0:
  9.7 38.4 all-gather.4
  50.9 53.7 all-gather.6
  106.9 94.6 all-gather.8
  206.9 72.1 all-reduce.1
  306.5 37.9 reduce-scatter.1
where the time goes:
time: 354 us; the launch traced here: 353 us
  waiting for transfers between devices  220 us (62%)
  local copies, waits for them, and re-layouts  48.9 us (14%)
  matrix products  45.3 us (13%)
  other arithmetic  23.8 us (7%)
  between operations  14.7 us (4%)
    all_gather x1, waiting for transfers between devices, gather_packed(): gathered = lax.all_gather(joined, axis_name, axis=0, tiled=False)  65.2 us
    all_gather x1, waiting for transfers between devices, on_device(): w_qkv_full = lax.all_gather(w_qkv, 'req', axis=1, tiled=True)  53.4 us
    psum x1, waiting for transfers between devices, on_device(): lax.psum(partial_value.astype(jnp.bfloat16), 'mp').astype(jnp.float32)  41.3 us
    reduce_scatter x1, waiting for transfers between devices, on_device(): lax.psum_scatter(terms.astype(jnp.bfloat16), 'mp', scatter_dimension=1, t...  34.8 us
    all_gather x1, waiting for transfers between devices, on_device(): full_rows = lax.all_gather(hidden_in, 'mp', axis=1, tiled=True)  24.7 us
    dot_general x1, matrix products, on_device(): terms = jnp.dot(units, w_down_full, preferred_element_type=jnp.float32)  15.4 us
    another operation x2, local copies, waits for them, and re-layouts, gather_packed(): outs.append(piece.reshape(shape))  14.8 us
    unnamed x19, local copies, waits for them, and re-layouts  12.2 us
  transfers between devices with their start and end apart: 5, of which 5 were waited for; matrix products, arithmetic and copies ran while one was open for 23% of the time, Pallas kernels for 0%

commit v1 on v0

--- a/solution.py
+++ b/solution.py
@@ -7,6 +7,11 @@
 THETA = 130000.0
 EPSILON = 1e-05
 NEG_FILL = -1e30
+
+
+def gather_from_all(x, axis, dim):
+    copies = jnp.concatenate([x] * lax.axis_size(axis), axis=dim)
+    return lax.all_to_all(copies, axis, dim, dim, tiled=True)
 
 
 def rms_scale(rows, gain):
@@ -66,7 +71,7 @@
     hidden_in, w_qkv, w_out, attn_gain, mlp_gain, w_gate, w_up, w_down, k_cache, v_cache, cache_len
 ):
     new_count = hidden_in.shape[0]
-    w_qkv_full = lax.all_gather(w_qkv, "req", axis=1, tiled=True)
+    w_qkv_full = gather_from_all(w_qkv, "req", 1)
     w_gate_full, w_up_full, w_down_full, w_out_full = gather_packed(
         [w_gate, w_up, w_down, w_out], [0, 0, 1, 1], "req"
     )

time: 354 us -> 341 us (0.963)
  waiting for transfers between devices: 220 us -> 186 us
  local copies, waits for them, and re-layouts: 48.9 us -> 61 us
  starting transfers between devices: 0.42 us -> 8.91 us
    all_gather x1 -> x0, waiting for transfers between devices: 53.4 us -> none  [on_device(): w_qkv_full = lax.all_gather(w_qkv, 'req', axis=1, tiled=True)]
    all_to_all x0 -> x1, waiting for transfers between devices: none -> 51 us  [gather_from_all(): return lax.all_to_all(copies, axis, dim, dim, tiled=True)]
    all_gather x1, waiting for transfers between devices: 65.2 us -> 35.8 us  [gather_packed(): gathered = lax.all_gather(joined, axis_name, axis=0, tiled=False)]
    all_gather x1, waiting for transfers between devices: 24.7 us -> 3.79 us  [on_device(): full_rows = lax.all_gather(hidden_in, 'mp', axis=1, tiled=True)]
    psum x1, waiting for transfers between devices: 41.3 us -> 59.6 us  [on_device(): lax.psum(partial_value.astype(jnp.bfloat16), 'mp').astype(jnp.float32)]
    unnamed x19 -> x35, local copies, waits for them, and re-layouts: 12.2 us -> 23.7 us
    all_to_all x0 -> x1, starting transfers between devices: none -> 8.31 us  [gather_from_all(): return lax.all_to_all(copies, axis, dim, dim, tiled=True)]
  transfers between devices with their start and end apart: 5 -> 5, of which waited for: 5 -> 5; matrix products, arithmetic and copies ran while one was open for 23% -> 28% of each run, Pallas kernels for 0% -> 0%
where the time goes in v1:
time: 341 us; the launch traced here: 340 us
  waiting for transfers between devices  186 us (55%)
  local copies, waits for them, and re-layouts  61 us (18%)
  matrix products  45.7 us (13%)
  other arithmetic  23.8 us (7%)
  between operations  14.7 us (4%)
  starting transfers between devices  8.91 us (3%)
    psum x1, waiting for transfers between devices, on_device(): lax.psum(partial_value.astype(jnp.bfloat16), 'mp').astype(jnp.float32)  59.6 us
    all_to_all x1, waiting for transfers between devices, gather_from_all(): return lax.all_to_all(copies, axis, dim, dim, tiled=True)  51 us
    all_gather x1, waiting for transfers between devices, gather_packed(): gathered = lax.all_gather(joined, axis_name, axis=0, tiled=False)  35.8 us
    reduce_scatter x1, waiting for transfers between devices, on_device(): lax.psum_scatter(terms.astype(jnp.bfloat16), 'mp', scatter_dimension=1, t...  34.8 us
    unnamed x35, local copies, waits for them, and re-layouts  23.7 us
    dot_general x1, matrix products, on_device(): terms = jnp.dot(units, w_down_full, preferred_element_type=jnp.float32)  15.4 us
    another operation x2, local copies, waits for them, and re-layouts, gather_packed(): outs.append(piece.reshape(shape))  14.7 us
    slice x1, local copies, waits for them, and re-layouts, gather_packed(): piece = gathered[:, offset:offset + rows].reshape((count,) + block.shape)  9.01 us
  transfers between devices with their start and end apart: 5, of which 5 were waited for; matrix products, arithmetic and copies ran while one was open for 28% of the time, Pallas kernels for 0%

profile of v1, /device:TPU:0, one launch (start us, length us, event | category | flops | bytes accessed | tf_op | source)
XLA Modules:
  0.0 339.9 jit_solution(2906134873851448980)
XLA Ops:
  7.2 0.7 all-gather.4.cloned.1.call-update
  8.0 1.1 reshape.167
  9.0 1.1 reshape.168
  10.1 2.0 pad_maximum_fusion
  12.2 0.9 constant_dynamic-update-slice_fusion.15
  13.0 0.9 constant_dynamic-update-slice_fusion.14
  13.9 0.9 constant_dynamic-update-slice_fusion.13
  14.8 0.9 constant_dynamic-update-slice_fusion.12
  15.6 0.9 constant_dynamic-update-slice_fusion.11
  16.5 0.9 constant_dynamic-update-slice_fusion.10
  17.4 0.9 constant_dynamic-update-slice_fusion.9
  18.3 0.9 constant_dynamic-update-slice_fusion.8
  19.1 0.9 constant_dynamic-update-slice_fusion.7
  20.0 0.9 constant_dynamic-update-slice_fusion.6
  20.9 0.9 constant_dynamic-update-slice_fusion.5
  21.7 0.9 constant_dynamic-update-slice_fusion.4
  22.7 0.9 constant_dynamic-update-slice_fusion.3
  23.5 0.9 constant_dynamic-update-slice_fusion.2
  24.4 0.9 constant_dynamic-update-slice_fusion.1
  25.3 0.9 constant_dynamic-update-slice_fusion
  26.2 8.3 %all-to-all-start = ((bf16[3,2048,256]{2,0,1:T(4,128)(2,1)}), bf16[3,2048,256]{2,0,1:T(4,128)(2,1)}, u32[]{:S(2)}, u32[]{:S(2)}) async-start(bf16[3,2048,256]{2,0,1:T(4,128)(2,1)} %constant_dynamic-update-slice_fusion), calls=%async_computation | async-start | bytes 8388608 | tf_op jit(solution)/shard_map/all_to_all | solution.py:14
  34.5 0.2 all-reduce.2.cloned.1.call-start
  35.4 2.9 copy.101
  38.4 4.2 %copy.102 = bf16[1,4096,256]{1,2,0:T(8,128)(2,1)} copy(bf16[1,4096,256]{2,1,0:T(8,128)(2,1)} %param.22) | data formatting | bytes 4194304 | tf_op args[9]
  42.6 1.3 iota_compare_fusion
  43.9 0.5 multiply_cosine_fusion
  44.4 3.8 %all-gather.4.cloned.1.call-done = bf16[1024,2048]{1,0:T(8,128)(2,1)} async-done(((bf16[1024,256]{1,0:T(8,128)(2,1)}), bf16[1024,2048]{1,0:T(8,128)(2,1)}) %all-gather.4.cloned.1.call-update) | async-done | bytes 4194320 | tf_op jit(solution)/shard_map/all_gather | solution.py:81
  48.2 3.1 fusion.26
  51.3 51.0 %all-to-all-done = bf16[3,2048,256]{2,0,1:T(4,128)(2,1)} async-done(((bf16[3,2048,256]{2,0,1:T(4,128)(2,1)}), bf16[3,2048,256]{2,0,1:T(4,128)(2,1)}, u32[]{:S(2)}, u32[]{:S(2)}) %all-to-all-start) | async-done | bytes 3145760 | tf_op jit(solution)/shard_map/all_to_all | solution.py:14
  102.2 7.1 %fusion.39 = f32[3,1024,256]{1,2,0:T(8,128)S(1)} fusion(bf16[1024,2048]{1,0:T(8,128)(2,1)} %all-gather.4.cloned.1.call-done, f32[2048]{0:T(1024)S(1)} %convert_element_type.84, f32[1024]{0:T(1024)S(1)} %add_rsqrt_fusion.1, bf16[3,2048,256]{2,0,1:T(4,128)(2,1)} %all-to-all-done), kind=kOutput, calls=%fused_computation.53 | convolution fusion | flops 3229614080 | bytes 10498048 | tf_op jit(solution)/shard_map/nd,kdw->knw/dot_general | solution.py:84
  109.4 0.9 slice.66
  110.3 0.1 fusion.60
  110.4 0.2 subtract_convert_fusion
  110.6 0.2 multiply_subtract_fusion
  110.8 0.4 copy-done.4
  111.2 0.7 copy-done.2
  111.9 3.0 fusion.20
  114.9 4.2 %fusion.22 = f32[4,1024]{1,0:T(4,128)S(1)} fusion(f32[4,1024,1024]{1,2,0:T(8,128)S(1)} %get-tuple-element.105, f32[4,1024]{1,0:T(4,128)S(1)} %get-tuple-element.101, pred[1024,1024]{0,1:T(8,128)(4,1)S(1)} %copy-done.2), kind=kLoop, calls=%fused_computation.31 | loop fusion | flops 20967424 | bytes 17858560 | tf_op jit(solution)/shard_map/reduce_sum | solution.py:63
  119.2 6.0 %fusion.44 = f32[4,1024,64]{1,2,0:T(8,128)} fusion(bf16[1024,4,64]{0,2,1:T(8,128)(2,1)S(1)} %bitcast.90, f32[4,1024,1024]{1,2,0:T(8,128)S(1)} %get-tuple-element.105, f32[4,1024]{1,0:T(4,128)S(1)} %get-tuple-element.101, pred[1024,1024]{0,1:T(8,128)(4,1)S(1)} %copy-done.2, f32[4,1024]{1,0:T(4,128)S(1)} %get-tuple-element.99), kind=kOutput, calls=%fused_computation.54 | convolution fusion | flops 558104576 | bytes 19431424 | tf_op jit(solution)/shard_map/hqk,khd->hqd/dot_general | solution.py:64
  125.1 8.0 %while.14 = (s32[]{:T(128)}, f32[4,1024,1]{1,0,2:T(4,128)S(1)}, f32[4,1024,1]{1,0,2:T(4,128)S(1)}, f32[4,1024,64]{1,2,0:T(8,128)}, s32[]{:T(128)}, /*index=5*/s3...) while((s32[]{:T(128)}, f32[4,1024,1]{1,0,2:T(4,128)S(1)}, ...), condition=%wide.region_6.7_spmd, body=%wide.region_3.6_spmd.sunk | while | flops 564671488 | bytes 36965104 | solution.py:114
  125.1 0.7 add_compare_fusion.2
  125.8 1.6 bitcast_reduce_fusion.2
  127.4 3.1 fusion.79
  130.5 2.5 fusion.78
  133.1 1.3 divide_convert_fusion
  134.4 35.8 %all-gather.6.cloned.1.call-done = bf16[53248,128]{1,0:T(8,128)(2,1)} async-done(((bf16[3328,128]{1,0:T(8,128)(2,1)}), bf16[53248,128]{1,0:T(8,128)(2,1)}) %all-gather.6.cloned.1.call-update) | async-done | bytes 13631504 | tf_op jit(solution)/shard_map/all_gather | solution.py:40
  170.2 1.3 slice_bitcast_fusion.1
  171.5 0.5 copy.103
  172.1 3.3 convolution_convert_fusion
  175.4 0.3 reduce-scatter.2.cloned.1.call-start
  175.7 0.3 copy-done.9
  176.1 9.0 %fusion.59 = (bf16[16,1024,128]{2,1,0:T(8,128)(2,1)}, bf16[1024,16,128]{2,0,1:T(8,128)(2,1)}, bf16[16,1024,128]{2,1,0:T(8,128)(2,1)}) fusion(bf16[16,3328,128]{2,1,0:T(8,128)(2,1)} %bitcast.78), kind=kLoop, calls=%fused_computation.98 | loop fusion | bytes 25165824 | tf_op jit(solution)/shard_map/slice | solution.py:45
  185.1 7.4 %reshape_reshape.6 = bf16[2048,1024]{1,0:T(8,128)(2,1)} reshape(bf16[16,1024,128]{2,1,0:T(8,128)(2,1)} %get-tuple-element.92) | data formatting | bytes 8388608 | tf_op jit(solution)/shard_map/reshape;reshape | solution.py:49
  192.5 6.4 %copy.104 = bf16[1024,16,128]{0,2,1:T(8,128)(2,1)} copy(bf16[1024,16,128]{2,0,1:T(8,128)(2,1)} %get-tuple-element.91) | data formatting | bytes 8388608 | tf_op jit(solution)/shard_map/transpose | solution.py:46
  198.9 7.3 %reshape_reshape.7 = bf16[2048,1024]{1,0:T(8,128)(2,1)} reshape(bf16[16,1024,128]{2,1,0:T(8,128)(2,1)} %get-tuple-element.90) | data formatting | bytes 8388608 | tf_op jit(solution)/shard_map/reshape;reshape | solution.py:49
  206.2 59.6 %all-reduce.2.cloned.1.call-done = bf16[1024,2048]{1,0:T(8,128)(2,1)} async-done(((bf16[1024,2048]{1,0:T(8,128)(2,1)}), bf16[1024,2048]{1,0:T(8,128)(2,1)}) %all-reduce.2.cloned.1.call-update) | async-done | bytes 4194320 | tf_op jit(solution)/shard_map/psum | solution.py:117
  265.8 5.6 %fusion.23 = (f32[1024]{0:T(1024)S(1)}, bf16[1024,2048]{1,0:T(8,128)(2,1)S(1)}) fusion(bf16[1024,2048]{1,0:T(8,128)(2,1)} %all-reduce.2.cloned.1.call-done, bf16[1024,2048]{1,0:T(8,128)(2,1)} %all-gather.4.cloned.1.call-done), kind=kLoop, calls=%fused_computation.34 | loop fusion | flops 14679040 | bytes 12587008 | tf_op jit(solution)/shard_map/reduce_sum | solution.py:19
  271.4 6.3 %fusion.48 = f32[1024,1024]{1,0:T(8,128)} fusion(bf16[2048,1024]{1,0:T(8,128)(2,1)S(1)} %copy-done.3, bf16[1024,2048]{1,0:T(8,128)(2,1)S(1)} %get-tuple-element.87, f32[2048]{0:T(1024)S(1)} %convert_element_type.99, f32[1024]{0:T(1024)S(1)} %add_rsqrt_fusion), kind=kOutput, calls=%fused_computation.55 | convolution fusion | flops 4303355904 | bytes 12595200 | tf_op jit(solution)/shard_map/dot_general | solution.py:123
  277.7 15.4 %convolution_convert_fusion.1 = bf16[1024,2048]{1,0:T(8,128)(2,1)} fusion(bf16[1024,2048]{0,1:T(8,128)(2,1)} %bitcast.83, f32[1024,1024]{1,0:T(8,128)} %fusion.48, bf16[2048,1024]{1,0:T(8,128)(2,1)} %reshape_reshape.7, bf16[1024,2048]{1,0:T(8,128)(2,1)} %copy-done.1, f32[2048]{0:T(1024)S(1)} %convert_element_type.99, f32[1024]{0:T(1024)S(1)} %add_rsqrt_fusion), kind=kOutput, calls=%fused_computation.51 | convolution fusion | flops 8606711808 | bytes 20983808 | tf_op jit(solution)/shard_map/dot_general | solution.py:126
  293.2 1.0 copy.105
  294.2 1.3 slice_bitcast_fusion.2
  295.5 1.0 copy.106
  296.5 34.8 %reduce-scatter.2.cloned.1.call-done = bf16[1024,256]{1,0:T(8,128)(2,1)} async-done(((bf16[1024,2048]{1,0:T(8,128)(2,1)}), bf16[1024,256]{1,0:T(8,128)(2,1)}) %reduce-scatter.2.cloned.1.call-update) | async-done | bytes 524304 | tf_op jit(solution)/shard_map/reduce_scatter | solution.py:127
  331.2 2.1 add_convert_fusion
  (35 shorter events, 0.3 us)
Async XLA Ops:
  7.2 5.0 %copy-start = (bf16[3,128,256]{2,1,0:T(8,128)(2,1)S(1)}, bf16[3,128,256]{2,1,0:T(8,128)(2,1)}, u32[]{:S(2)}) copy-start(bf16[3,128,256]{2,1,0:T(8,128)(2,1)} %param.14) | copy-start | bytes 589828
  7.2 41.0 %all-gather.4.cloned.1.call-start = ((), (), s32[]{:S(2)}) async-start(), calls=%async_computation.2 | async-start | bytes 4718592 | tf_op jit(solution)/shard_map/all_gather | solution.py:81
  7.9 162.3 %all-gather.6.cloned.1.call-start = ((), (), s32[]{:S(2)}) async-start(), calls=%async_computation.5 | async-start | bytes 14483456 | tf_op jit(solution)/shard_map/all_gather | solution.py:40
  26.2 9.2 %copy-start.8 = (bf16[2048]{0:T(1024)(128)(2,1)S(1)}, bf16[2048]{0:T(1024)(128)(2,1)}, u32[]{:S(2)}) copy-start(bf16[2048]{0:T(1024)(128)(2,1)} %param.16) | copy-start | bytes 12292
  26.2 76.0 %all-to-all-start = ((bf16[3,2048,256]{2,0,1:T(4,128)(2,1)}), bf16[3,2048,256]{2,0,1:T(4,128)(2,1)}, u32[]{:S(2)}, u32[]{:S(2)}) async-start(bf16[3,2048,256]{2,0,1:T(4,128)(2,1)} %constant_dynamic-update-slice_fusion), calls=%async_computation | async-start | bytes 8388608 | tf_op jit(solution)/shard_map/all_to_all | solution.py:14
  34.5 231.3 %all-reduce.2.cloned.1.call-start = ((), (), s32[]{:S(2)}) async-start(), calls=%async_computation.3 | async-start | bytes 8388608 | tf_op jit(solution)/shard_map/psum | solution.py:117
  109.4 1.8 copy-start.4
  110.3 1.6 copy-start.2
  114.9 4.2 %copy-start.7 = (bf16[1,1024,256]{1,2,0:T(8,128)(2,1)S(1)}, bf16[1,1024,256]{1,2,0:T(8,128)(2,1)}, u32[]{:S(2)}) copy-start(bf16[1,1024,256]{1,2,0:T(8,128)(2,1)} %slice.66) | copy-start | bytes 1572868
  125.8 1.6 copy-start.5
  130.5 2.6 copy-start.6
  175.4 0.7 copy-start.9
  175.4 155.8 %reduce-scatter.2.cloned.1.call-start = ((), (), s32[]{:S(2)}) async-start(), calls=%async_computation.4 | async-start | bytes 4718592 | tf_op jit(solution)/shard_map/reduce_scatter | solution.py:127
  265.8 5.6 %copy-start.3 = (bf16[2048,1024]{1,0:T(8,128)(2,1)S(1)}, bf16[2048,1024]{1,0:T(8,128)(2,1)}, u32[]{:S(2)}) copy-start(bf16[2048,1024]{1,0:T(8,128)(2,1)} %reshape_reshape.6) | copy-start | bytes 12582916
  271.4 6.4 %copy-start.1 = (bf16[1024,2048]{1,0:T(8,128)(2,1)}, bf16[1024,2048]{1,0:T(8,128)(2,1)S(1)}, u32[]{:S(2)}) copy-start(bf16[1024,2048]{1,0:T(8,128)(2,1)S(1)} %get-tuple-element.87) | copy-start | bytes 12582916
Sparse Core Ops, SparseCore 0:
  9.7 38.4 all-gather.3
  50.4 119.7 all-gather.5
  175.6 90.1 all-reduce.1
  293.3 37.9 reduce-scatter.1
